TPU v7x, 32 devices: a whole 2x2x4 slice. The times are simulated.
32 devices in a mesh: vol: 8 (over z, y), ptcl: 4 (over x, core).
Axes of the slice: x: 2, y: 2, z: 4, core: 2. Of those that a mesh axis runs over, the one named last changes fastest.
Arguments:
- images: bfloat16 [32, 256, 256], P(('vol', 'ptcl')), may hold values from -6 to 6
- defocus: bfloat16 [32], P(('vol', 'ptcl')), may hold values from 20 to 200
- volume: float32 [4096, 256], P('vol'), may hold values from -6 to 6
- counts: int32 [8, 4, 8], P('vol', 'ptcl'), may hold values from 1 to 96, as said below
- slot_pixel: int32 [8, 4, 8, 96], P('vol', 'ptcl'), may hold values from 0 to 511, as said below
- slot_taps: int32 [8, 4, 8, 8, 96], P('vol', 'ptcl'), may hold values from 0 to 511, as said below
- slot_weights: bfloat16 [8, 4, 8, 8, 96], P('vol', 'ptcl'), may hold values from 0.019897461 to 0.25
Outputs:
- volume_next: float32 [4096, 256], P('vol')
Inputs may be any that keep to these rules, and one draw needn't show every extreme that they name: The 8 counts of each holder sum to 512; in each particle shard one owner receives exactly 96 live slots from every holder of that shard. `slot_pixel`: the live slots of a holder (slot index below its count) name each of its 512 pixel blocks exactly once; the other slots hold valid ids. `slot_taps`: the 8 taps of one slot name 8 different blocks.
All inputs are finite; a program needn't handle non-finite values.
Results may differ from a plain program's by a relative error of at most 0.0034.
Values may be sent and summed in bfloat16 or wider, within the bound.
No kernel may reach another device: no remote copies, remote signals or barrier semaphores. Data moves between devices by JAX's collectives and lax.ppermute only.
A program may use at most 64 MiB of HBM per device.

v0:
```python
import math
import jax
import jax.numpy as jnp
from jax import lax
from jax.sharding import PartitionSpec as P

L = 256
BLK = 128
PB = 512
learn_rate = 1.0
phase_shift = 0.1


def dft_tables():
    freq_ids = jnp.arange(L, dtype=jnp.int32)
    product = (freq_ids[:, None] - L // 2) * freq_ids[None, :] % L
    angle = 2.0 * math.pi / L * product.astype(jnp.float32)
    return (jnp.cos(angle).astype(jnp.bfloat16), jnp.sin(angle).astype(jnp.bfloat16))


def transform(pictures, cos_table, sin_table):
    first = jnp.stack([cos_table, sin_table])
    rows = jnp.einsum("iyx,jkx->ijyk", pictures, first, preferred_element_type=jnp.float32).astype(
        jnp.bfloat16
    )
    count_img = pictures.shape[0]
    rows = rows.reshape(count_img, 2 * L, L)
    scale = jnp.asarray(1.0 / L, jnp.bfloat16)
    second = (
        jnp.concatenate(
            [
                jnp.concatenate([cos_table, -sin_table], axis=1),
                jnp.concatenate([-sin_table, -cos_table], axis=1),
            ],
            axis=0,
        )
        * scale
    )
    parts = jnp.einsum("ay,iyb->iab", second, rows, preferred_element_type=jnp.float32)
    parts = parts.reshape(count_img, 2, L, L // BLK, BLK)
    blocks = jnp.transpose(parts, (0, 2, 3, 1, 4))
    return blocks.reshape(count_img * PB, 2 * BLK).astype(jnp.bfloat16)


def ctf_rows(block_id, focus):
    row_id = block_id // (L // BLK)
    col_id = block_id % (L // BLK) * BLK
    lane_ids = jnp.arange(BLK, dtype=jnp.int32)
    freq_y = (row_id - L // 2).astype(jnp.float32) / L
    freq_x = (col_id[..., None] + lane_ids - L // 2).astype(jnp.float32) / L
    radius = freq_x * freq_x + (freq_y * freq_y)[..., None]
    return -jnp.sin(math.pi * focus.astype(jnp.float32)[..., None] * radius + phase_shift)


def residual_terms(prediction, observed, ctf_values, live_slots):
    shape = prediction.shape
    pred_wide = prediction.astype(jnp.float32).reshape(shape[:-1] + (2, BLK))
    obs_wide = observed.astype(jnp.float32).reshape(shape[:-1] + (2, BLK))
    factor = ctf_values[..., None, :]
    misfit = factor * (factor * pred_wide - obs_wide)
    misfit = jnp.where(live_slots[..., None, None], misfit, 0.0)
    return misfit.reshape(shape).astype(jnp.bfloat16)


def tap_matrix(tap_ids, weights, block_count):
    owners, taps, slots = tap_ids.shape
    flat_taps = jnp.transpose(tap_ids, (0, 2, 1)).reshape(owners * slots, taps)
    flat_weights = jnp.transpose(weights, (0, 2, 1)).reshape(owners * slots, taps)
    block_ids = jnp.arange(block_count, dtype=jnp.int32)
    picked = jnp.where(
        flat_taps[:, :, None] == block_ids[None, None, :],
        flat_weights[:, :, None],
        jnp.zeros((), jnp.bfloat16),
    )
    return jnp.sum(picked, axis=1, dtype=jnp.bfloat16)


def local(images, defocus, volume, counts, slot_pixel, slot_taps, slot_weights):
    cos_table, sin_table = dft_tables()
    extract = volume.astype(jnp.bfloat16)
    slot_count = counts[0, 0]
    pixel_ids = slot_pixel[0, 0]
    tap_ids = slot_taps[0, 0]
    weights = slot_weights[0, 0]
    owners, taps, capacity = tap_ids.shape
    live_slots = jnp.arange(capacity, dtype=jnp.int32)[None, :] < slot_count[:, None]
    meta = jnp.concatenate(
        [
            tap_ids.astype(jnp.float32),
            weights.astype(jnp.float32),
            (pixel_ids % PB).astype(jnp.float32)[:, None, :],
            defocus[pixel_ids // PB].astype(jnp.float32)[:, None, :],
            live_slots.astype(jnp.float32)[:, None, :],
        ],
        axis=1,
    )
    got_meta = lax.all_to_all(meta, "vol", split_axis=0, concat_axis=0, tiled=True)
    observed = transform(images, cos_table, sin_table)
    rows = observed[pixel_ids]
    got_rows = lax.all_to_all(rows, "vol", split_axis=0, concat_axis=0, tiled=True)
    got_taps = got_meta[:, :taps, :].astype(jnp.int32)
    got_weights = got_meta[:, taps : 2 * taps, :].astype(jnp.bfloat16)
    got_block = got_meta[:, 2 * taps, :].astype(jnp.int32)
    got_focus = got_meta[:, 2 * taps + 1, :]
    got_live = got_meta[:, 2 * taps + 2, :] > 0.5
    matrix = tap_matrix(got_taps, got_weights, volume.shape[0])
    prediction = jnp.dot(matrix, extract, preferred_element_type=jnp.float32)
    prediction = prediction.astype(jnp.bfloat16).reshape(owners, capacity, -1)
    ctf_values = ctf_rows(got_block, got_focus)
    weighted = residual_terms(prediction, got_rows, ctf_values, got_live)
    flat_residual = weighted.reshape(-1, volume.shape[1])
    gradient = lax.dot_general(
        matrix, flat_residual, (((0,), (0,)), ((), ())), preferred_element_type=jnp.float32
    )
    gradient = lax.psum(gradient, "ptcl")
    return volume - learn_rate * gradient


def solution(mesh):
    placed = (
        P(("vol", "ptcl"), None, None),
        P(("vol", "ptcl")),
        P("vol", None),
        P("vol", "ptcl", None),
        P("vol", "ptcl", None, None),
        P("vol", "ptcl", None, None, None),
        P("vol", "ptcl", None, None, None),
    )
    return jax.shard_map(
        local, mesh=mesh, in_specs=placed, out_specs=P("vol", None), check_vma=False
    )
```

profile of v0, /device:TPU:0, one launch (start us, length us, event | category | flops | bytes accessed | tf_op | source)
XLA Modules:
  0.0 89.9 jit_solution(17016676902778621159)
XLA Ops:
  7.2 0.7 compare_convert_fusion
  8.0 0.7 fusion.40
  8.7 0.8 convert_bitcast_fusion
  9.4 0.7 bitcast_convert_fusion
  10.2 1.9 %concatenate.12 = f32[8,19,96]{2,1,0:T(8,128)} concatenate(f32[8,8,96]{2,1,0:T(8,128)S(1)} %convert_bitcast_fusion, f32[8,8,96]{2,1,0:T(8,128)S(1)} %bitcast_convert_fusion, f32[8,1,96]{2,1,0:T(1,128)S(1)} %fusion.40, f32[8,1,96]{2,1,0:T(1,128)S(1)} %gather.6, f32[8,1,96]{2,1,0:T(1,128)S(1)} %compare_convert_fusion), dimensions={1} | concatenate | bytes 116736 | tf_op jit(solution)/shard_map/concatenate | solution.py:87
  12.0 7.3 %all-to-all-start = ((f32[8,19,96]{2,1,0:T(8,128)}), f32[8,19,96]{2,1,0:T(8,128)S(1)}, u32[]{:S(2)}, u32[]{:S(2)}) async-start(f32[8,19,96]{2,1,0:T(8,128)} %concatenate.12), calls=%async_computation | async-start | bytes 196608 | tf_op jit(solution)/shard_map/all_to_all | solution.py:97
  19.3 0.7 compare_select_fusion.2
  20.0 1.1 %cosine_convert_fusion = bf16[256,256]{1,0:T(8,128)(2,1)S(1)} fusion(s32[256]{0:T(256)S(1)} %iota_add_fusion), kind=kLoop, calls=%fused_computation.39 | loop fusion | flops 983040 | bytes 132096 | tf_op jit(solution)/shard_map/convert_element_type | solution.py:18
  21.1 1.3 %fusion.30 = (bf16[256,256]{1,0:T(8,128)(2,1)S(1)}, bf16[256,256]{1,0:T(8,128)(2,1)S(1)}) fusion(s32[256]{0:T(256)S(1)} %iota_add_fusion), kind=kLoop, calls=%fused_computation.49 | loop fusion | flops 1441792 | bytes 263168 | tf_op jit(solution)/shard_map/neg | solution.py:32
  22.4 1.3 %cosine_convert_fusion.1 = (bf16[1,256,256]{2,1,0:T(8,128)(2,1)S(1)}, bf16[1,256,256]{2,1,0:T(8,128)(2,1)S(1)}) fusion(s32[256]{0:T(256)S(1)} %iota_add_fusion), kind=kLoop, calls=%fused_computation.43 | loop fusion | flops 1048576 | bytes 263168 | tf_op jit(solution)/shard_map/convert_element_type | solution.py:18
  23.6 0.1 reshape.345
  23.7 0.3 convolution_convert_fusion.2
  24.0 0.4 fusion.2
  24.3 0.1 convert_element_type.192
  24.4 0.5 copy.25
  25.0 3.3 %gather_fusion = bf16[768,256]{1,0:T(8,128)(2,1)} fusion(bf16[512,256]{1,0:T(8,128)(2,1)S(1)} %bitcast.54, s32[1024]{0:T(1024)S(1)} %pad_clamp_fusion), kind=kCustom, calls=%fused_computation | custom fusion | bytes 789504 | tf_op jit(solution)/shard_map/gather | solution.py:99
  28.2 6.0 %all-to-all-start.1 = ((bf16[8,96,256]{2,1,0:T(8,128)(2,1)}), bf16[8,96,256]{2,1,0:T(8,128)(2,1)S(1)}, u32[]{:S(2)}, u32[]{:S(2)}) async-start(bf16[8,96,256]{2,1,0:T(8,128)(2,1)} %bitcast.22), calls=%async_computation.1 | async-start | bytes 786432 | tf_op jit(solution)/shard_map/all_to_all | solution.py:100
  34.2 0.0 all-reduce.2.cloned.1.call-start
  34.3 0.1 copy.27
  34.5 0.2 copy.26
  34.7 5.1 %fusion.1 = bf16[768,512]{1,0:T(8,128)(2,1)S(1)} fusion(s32[768,8]{1,0:T(8,128)S(1)} %bitcast.56, bf16[768,8]{1,0:T(8,128)(2,1)S(1)} %bitcast.59), kind=kLoop, calls=%fused_computation.3 | loop fusion | flops 9043968 | bytes 823296 | tf_op jit(solution)/shard_map/reduce_sum | solution.py:75
  39.7 3.6 %sine_negate_fusion = f32[8,96,128]{2,1,0:T(8,128)S(1)} fusion(f32[8,96]{1,0:T(8,128)S(1)} %fusion.39, s32[8,96]{1,0:T(8,128)S(1)} %fusion.35, f32[8,96]{1,0:T(8,128)S(1)} %bitcast.63), kind=kLoop, calls=%fused_computation.26 | loop fusion | flops 884736 | bytes 402432 | tf_op jit(solution)/shard_map/neg | solution.py:52
  43.3 0.3 mul.162
  43.6 0.6 mul.163
  44.3 0.4 copy-done.1
  44.6 0.4 convolution_convert_fusion
  45.0 0.3 all-to-all-done.1
  45.4 0.2 fusion.6
  45.5 1.2 %fusion.48 = f32[512,256]{1,0:T(8,128)} fusion(bf16[768,512]{1,0:T(8,128)(2,1)S(1)} %fusion.1, bf16[768,256]{1,0:T(8,128)(2,1)S(1)} %bitcast.60), kind=kOutput, calls=%fused_computation.87 | convolution fusion | flops 201326592 | bytes 1703936 | tf_op jit(solution)/shard_map/dot_general | solution.py:112
  46.7 0.0 all-reduce.2.cloned.1.call-update
  46.8 34.4 %all-reduce.2.cloned.1.call-done = f32[512,256]{1,0:T(8,128)} async-done(((f32[512,256]{1,0:T(8,128)}), f32[512,256]{1,0:T(8,128)}) %all-reduce.2.cloned.1.call-update) | async-done | bytes 524304 | tf_op jit(solution)/shard_map/psum | solution.py:115
  81.2 1.9 %sub.41 = f32[512,256]{1,0:T(8,128)} subtract(f32[512,256]{1,0:T(8,128)S(1)} %copy-done.1, f32[512,256]{1,0:T(8,128)} %all-reduce.2.cloned.1.call-done) | non-fusion elementwise | flops 131072 | bytes 1572864 | tf_op jit(solution)/shard_map/sub | solution.py:116
  (14 shorter events, 0.1 us)
Async XLA Ops:
  6.5 17.2 %copy-start = (bf16[1,256,256]{2,1,0:T(8,128)(2,1)S(1)}, bf16[1,256,256]{2,1,0:T(8,128)(2,1)}, u32[]{:S(2)}) copy-start(bf16[1,256,256]{2,1,0:T(8,128)(2,1)} %param.7) | copy-start | bytes 393220
  12.0 16.2 %all-to-all-start = ((f32[8,19,96]{2,1,0:T(8,128)}), f32[8,19,96]{2,1,0:T(8,128)S(1)}, u32[]{:S(2)}, u32[]{:S(2)}) async-start(f32[8,19,96]{2,1,0:T(8,128)} %concatenate.12), calls=%async_computation | async-start | bytes 196608 | tf_op jit(solution)/shard_map/all_to_all | solution.py:97
  28.2 17.1 %all-to-all-start.1 = ((bf16[8,96,256]{2,1,0:T(8,128)(2,1)}), bf16[8,96,256]{2,1,0:T(8,128)(2,1)S(1)}, u32[]{:S(2)}, u32[]{:S(2)}) async-start(bf16[8,96,256]{2,1,0:T(8,128)(2,1)} %bitcast.22), calls=%async_computation.1 | async-start | bytes 786432 | tf_op jit(solution)/shard_map/all_to_all | solution.py:100
  34.2 46.9 %all-reduce.2.cloned.1.call-start = ((), (), s32[]{:S(2)}) async-start(), calls=%async_computation.2 | async-start | bytes 1048576 | tf_op jit(solution)/shard_map/psum | solution.py:115
  43.6 1.0 %copy-start.1 = (f32[512,256]{1,0:T(8,128)S(1)}, f32[512,256]{1,0:T(8,128)}, u32[]{:S(2)}) copy-start(f32[512,256]{1,0:T(8,128)} %param.9) | copy-start | bytes 1572868
Sparse Core Ops, SparseCore 0:
  46.9 34.2 all-reduce.1
where the time goes:
time: 90.5 us; the launch traced here: 89.9 us
  waiting for transfers between devices  34.8 us (38%)
  other arithmetic  18 us (20%)
  between operations  14.3 us (16%)
  starting transfers between devices  13.3 us (15%)
  local copies, waits for them, and re-layouts  7.42 us (8%)
  matrix products  2.18 us (2%)
    psum x1, waiting for transfers between devices, local(): gradient = lax.psum(gradient, 'ptcl')  34.4 us
    all_to_all x1, starting transfers between devices, local(): lax.all_to_all(meta, 'vol', split_axis=0, concat_axis=0, tiled=True)  7.28 us
    all_to_all x1, starting transfers between devices, local(): lax.all_to_all(rows, 'vol', split_axis=0, concat_axis=0, tiled=True)  5.99 us
    reduce_sum x1, other arithmetic, tap_matrix(): return jnp.sum(picked, axis=1, dtype=jnp.bfloat16)  5.06 us
    neg x1, other arithmetic, ctf_rows(): -jnp.sin(math.pi * focus.astype(jnp.float32)[..., None] * radius + phase_...  3.56 us
    gather x1, local copies, waits for them, and re-layouts, local(): rows = observed[pixel_ids]  3.28 us
    convert_element_type x2, other arithmetic, dft_tables(): jnp.cos(angle).astype(jnp.bfloat16)  2.31 us
    sub x1, other arithmetic, local(): return volume - learn_rate * gradient  1.9 us
  transfers between devices with their start and end apart: 3, of which 2 were waited for; matrix products, arithmetic and copies ran while one was open for 21% of the time, Pallas kernels for 0%

commit v1 on v0

--- a/solution.py
+++ b/solution.py
@@ -9,6 +9,11 @@
 PB = 512
 learn_rate = 1.0
 phase_shift = 0.1
+
+
+def add_all(value, axis):
+    parts = lax.all_gather(value, axis)
+    return jnp.sum(parts, axis=0)
 
 
 def dft_tables():
@@ -112,7 +117,7 @@
     gradient = lax.dot_general(
         matrix, flat_residual, (((0,), (0,)), ((), ())), preferred_element_type=jnp.float32
     )
-    gradient = lax.psum(gradient, "ptcl")
+    gradient = add_all(gradient, "ptcl")
     return volume - learn_rate * gradient
 
 

time: 90.5 us -> 80.2 us (0.89)
  waiting for transfers between devices: 34.8 us -> 24.1 us
    psum x1 -> x0, waiting for transfers between devices: 34.4 us -> none  [local(): gradient = lax.psum(gradient, 'ptcl')]
    all_gather x0 -> x1, waiting for transfers between devices: none -> 23.4 us  [add_all(): parts = lax.all_gather(value, axis)]
    reduce_sum x0 -> x1, other arithmetic: none -> 1.79 us  [add_all(): return jnp.sum(parts, axis=0)]
    sub x1, other arithmetic: 1.9 us -> 0.86 us  [local(): return volume - learn_rate * gradient]
  transfers between devices with their start and end apart: 3 -> 3, of which waited for: 2 -> 2; matrix products, arithmetic and copies ran while one was open for 21% -> 24% of each run, Pallas kernels for 0% -> 0%
where the time goes in v1:
time: 80.2 us; the launch traced here: 79.7 us
  waiting for transfers between devices  24.1 us (30%)
  other arithmetic  18.7 us (23%)
  between operations  14.3 us (18%)
  starting transfers between devices  13.3 us (17%)
  local copies, waits for them, and re-layouts  7.04 us (9%)
  matrix products  2.18 us (3%)
    all_gather x1, waiting for transfers between devices, add_all(): parts = lax.all_gather(value, axis)  23.4 us
    all_to_all x1, starting transfers between devices, local(): lax.all_to_all(meta, 'vol', split_axis=0, concat_axis=0, tiled=True)  7.28 us
    all_to_all x1, starting transfers between devices, local(): lax.all_to_all(rows, 'vol', split_axis=0, concat_axis=0, tiled=True)  5.99 us
    reduce_sum x1, other arithmetic, tap_matrix(): return jnp.sum(picked, axis=1, dtype=jnp.bfloat16)  5.06 us
    neg x1, other arithmetic, ctf_rows(): -jnp.sin(math.pi * focus.astype(jnp.float32)[..., None] * radius + phase_...  3.56 us
    gather x1, local copies, waits for them, and re-layouts, local(): rows = observed[pixel_ids]  3.28 us
    convert_element_type x2, other arithmetic, dft_tables(): jnp.cos(angle).astype(jnp.bfloat16)  2.31 us
    concatenate x1, local copies, waits for them, and re-layouts, local(): jnp.concatenate([tap_ids.astype(jnp.float32), weights.astype(jnp.float32)...  1.87 us
  transfers between devices with their start and end apart: 3, of which 2 were waited for; matrix products, arithmetic and copies ran while one was open for 24% of the time, Pallas kernels for 0%

profile of v1, /device:TPU:0, one launch (start us, length us, event | category | flops | bytes accessed | tf_op | source)
XLA Modules:
  0.0 79.7 jit_solution(8814417764922895563)
XLA Ops:
  7.2 0.7 compare_convert_fusion
  8.0 0.7 fusion.40
  8.7 0.8 convert_bitcast_fusion
  9.4 0.7 bitcast_convert_fusion
  10.2 1.9 %concatenate.12 = f32[8,19,96]{2,1,0:T(8,128)} concatenate(f32[8,8,96]{2,1,0:T(8,128)S(1)} %convert_bitcast_fusion, f32[8,8,96]{2,1,0:T(8,128)S(1)} %bitcast_convert_fusion, f32[8,1,96]{2,1,0:T(1,128)S(1)} %fusion.40, f32[8,1,96]{2,1,0:T(1,128)S(1)} %gather.6, f32[8,1,96]{2,1,0:T(1,128)S(1)} %compare_convert_fusion), dimensions={1} | concatenate | bytes 116736 | tf_op jit(solution)/shard_map/concatenate | solution.py:92
  12.0 7.3 %all-to-all-start = ((f32[8,19,96]{2,1,0:T(8,128)}), f32[8,19,96]{2,1,0:T(8,128)S(1)}, u32[]{:S(2)}, u32[]{:S(2)}) async-start(f32[8,19,96]{2,1,0:T(8,128)} %concatenate.12), calls=%async_computation | async-start | bytes 196608 | tf_op jit(solution)/shard_map/all_to_all | solution.py:102
  19.3 0.7 compare_select_fusion.2
  20.0 1.1 %cosine_convert_fusion = bf16[256,256]{1,0:T(8,128)(2,1)S(1)} fusion(s32[256]{0:T(256)S(1)} %iota_add_fusion), kind=kLoop, calls=%fused_computation.39 | loop fusion | flops 983040 | bytes 132096 | tf_op jit(solution)/shard_map/convert_element_type | solution.py:23
  21.1 1.3 %fusion.30 = (bf16[256,256]{1,0:T(8,128)(2,1)S(1)}, bf16[256,256]{1,0:T(8,128)(2,1)S(1)}) fusion(s32[256]{0:T(256)S(1)} %iota_add_fusion), kind=kLoop, calls=%fused_computation.49 | loop fusion | flops 1441792 | bytes 263168 | tf_op jit(solution)/shard_map/neg | solution.py:37
  22.4 1.3 %cosine_convert_fusion.1 = (bf16[1,256,256]{2,1,0:T(8,128)(2,1)S(1)}, bf16[1,256,256]{2,1,0:T(8,128)(2,1)S(1)}) fusion(s32[256]{0:T(256)S(1)} %iota_add_fusion), kind=kLoop, calls=%fused_computation.43 | loop fusion | flops 1048576 | bytes 263168 | tf_op jit(solution)/shard_map/convert_element_type | solution.py:23
  23.6 0.1 reshape.345
  23.7 0.3 convolution_convert_fusion.2
  24.0 0.4 fusion.2
  24.3 0.1 convert_element_type.192
  24.4 0.5 copy.25
  25.0 3.3 %gather_fusion = bf16[768,256]{1,0:T(8,128)(2,1)} fusion(bf16[512,256]{1,0:T(8,128)(2,1)S(1)} %bitcast.55, s32[1024]{0:T(1024)S(1)} %pad_clamp_fusion), kind=kCustom, calls=%fused_computation | custom fusion | bytes 789504 | tf_op jit(solution)/shard_map/gather | solution.py:104
  28.2 6.0 %all-to-all-start.1 = ((bf16[8,96,256]{2,1,0:T(8,128)(2,1)}), bf16[8,96,256]{2,1,0:T(8,128)(2,1)S(1)}, u32[]{:S(2)}, u32[]{:S(2)}) async-start(bf16[8,96,256]{2,1,0:T(8,128)(2,1)} %bitcast.22), calls=%async_computation.1 | async-start | bytes 786432 | tf_op jit(solution)/shard_map/all_to_all | solution.py:105
  34.2 0.0 all-gather.3.cloned.1.call-start
  34.3 0.1 copy.27
  34.5 0.2 copy.26
  34.7 5.1 %fusion.1 = bf16[768,512]{1,0:T(8,128)(2,1)S(1)} fusion(s32[768,8]{1,0:T(8,128)S(1)} %bitcast.58, bf16[768,8]{1,0:T(8,128)(2,1)S(1)} %bitcast.61), kind=kLoop, calls=%fused_computation.3 | loop fusion | flops 9043968 | bytes 823296 | tf_op jit(solution)/shard_map/reduce_sum | solution.py:80
  39.8 3.6 %sine_negate_fusion = f32[8,96,128]{2,1,0:T(8,128)S(1)} fusion(f32[8,96]{1,0:T(8,128)S(1)} %fusion.39, s32[8,96]{1,0:T(8,128)S(1)} %fusion.35, f32[8,96]{1,0:T(8,128)S(1)} %bitcast.65), kind=kLoop, calls=%fused_computation.26 | loop fusion | flops 884736 | bytes 402432 | tf_op jit(solution)/shard_map/neg | solution.py:57
  43.3 0.3 mul.162
  43.6 0.6 mul.163
  44.3 0.4 convolution_convert_fusion
  44.6 0.7 all-to-all-done.1
  45.4 0.2 fusion.6
  45.5 1.2 %fusion.48 = f32[512,256]{1,0:T(8,128)} fusion(bf16[768,512]{1,0:T(8,128)(2,1)S(1)} %fusion.1, bf16[768,256]{1,0:T(8,128)(2,1)S(1)} %bitcast.62), kind=kOutput, calls=%fused_computation.87 | convolution fusion | flops 201326592 | bytes 1703936 | tf_op jit(solution)/shard_map/dot_general | solution.py:117
  46.7 0.0 all-gather.3.cloned.1.call-update
  46.8 23.4 %all-gather.3.cloned.1.call-done = f32[2048,256]{1,0:T(8,128)} async-done(((f32[512,256]{1,0:T(8,128)}), f32[2048,256]{1,0:T(8,128)}) %all-gather.3.cloned.1.call-update) | async-done | bytes 2097168 | tf_op jit(solution)/shard_map/all_gather | solution.py:15
  70.2 1.8 %reduce_sum.19 = f32[512,256]{1,0:T(8,128)S(1)} reduce(f32[4,512,256]{2,1,0:T(8,128)} %bitcast.56, f32[]{:T(128)} %constant.88.clone.1), dimensions={0}, to_apply=%region_1.2 | reduce | flops 393216 | bytes 2621444 | tf_op jit(solution)/shard_map/reduce_sum | solution.py:16
  72.0 0.9 %sub.41 = f32[512,256]{1,0:T(8,128)} subtract(f32[512,256]{1,0:T(8,128)S(1)} %copy-done.1, f32[512,256]{1,0:T(8,128)S(1)} %reduce_sum.19) | non-fusion elementwise | flops 131072 | bytes 1572864 | tf_op jit(solution)/shard_map/sub | solution.py:121
  (15 shorter events, 0.1 us)
Async XLA Ops:
  6.5 17.2 %copy-start = (bf16[1,256,256]{2,1,0:T(8,128)(2,1)S(1)}, bf16[1,256,256]{2,1,0:T(8,128)(2,1)}, u32[]{:S(2)}) copy-start(bf16[1,256,256]{2,1,0:T(8,128)(2,1)} %param.7) | copy-start | bytes 393220
  12.0 16.2 %all-to-all-start = ((f32[8,19,96]{2,1,0:T(8,128)}), f32[8,19,96]{2,1,0:T(8,128)S(1)}, u32[]{:S(2)}, u32[]{:S(2)}) async-start(f32[8,19,96]{2,1,0:T(8,128)} %concatenate.12), calls=%async_computation | async-start | bytes 196608 | tf_op jit(solution)/shard_map/all_to_all | solution.py:102
  28.2 17.1 %all-to-all-start.1 = ((bf16[8,96,256]{2,1,0:T(8,128)(2,1)}), bf16[8,96,256]{2,1,0:T(8,128)(2,1)S(1)}, u32[]{:S(2)}, u32[]{:S(2)}) async-start(bf16[8,96,256]{2,1,0:T(8,128)(2,1)} %bitcast.22), calls=%async_computation.1 | async-start | bytes 786432 | tf_op jit(solution)/shard_map/all_to_all | solution.py:105
  34.2 35.9 %all-gather.3.cloned.1.call-start = ((), (), s32[]{:S(2)}) async-start(), calls=%async_computation.2 | async-start | bytes 2621440 | tf_op jit(solution)/shard_map/all_gather | solution.py:15
  34.7 9.6 %copy-start.1 = (f32[512,256]{1,0:T(8,128)S(1)}, f32[512,256]{1,0:T(8,128)}, u32[]{:S(2)}) copy-start(f32[512,256]{1,0:T(8,128)} %param.9) | copy-start | bytes 1572868
Sparse Core Ops, SparseCore 0:
  46.9 23.2 all-gather.2
